TPU v7x, 32 devices: a whole 2x2x4 slice. The times are simulated.
32 devices in a mesh: grp: 2 (over y), row: 4 (over z), col: 2 (over x), vec: 2 (over core).
Axes of the slice: x: 2, y: 2, z: 4, core: 2. Of those that a mesh axis runs over, the one named last changes fastest.
Arguments:
- start: float32 [64, 2048], P('vec', ('grp', 'row')), parts along dimension 1, may hold values from -6 to 6
- tiles: bfloat16 [16, 32, 128, 128], P(('grp', 'row'), 'col'), parts along dimension 0, may hold values from -6 to 6
- pattern: int32 [16, 32], P(('grp', 'row')), parts along dimension 0, may hold values from 0 to 7
- counts: int32 [16], P(('grp', 'row')), parts along dimension 0, may hold values from 1 to 32
Outputs:
- basis: float32 [64, 2048], P('vec', ('grp', 'row')), parts along dimension 1
There are 2 independent parts, one for each index of `grp`. A program takes and returns all parts, laid end to end along the dimension named above; each array names one. Nothing has to cross between parts.
Inputs may be any that keep to these rules, and one draw needn't show every extreme that they name: pattern may name a block column more than once in a block row; such tiles add.
All inputs are finite; a program needn't handle non-finite values.
Results may differ from a plain program's by a relative error of at most 0.03.
Values may be sent and summed in bfloat16 or wider, within the bound.
No kernel may reach another device: no remote copies, remote signals or barrier semaphores. Data moves between devices by JAX's collectives and lax.ppermute only.
A program may use at most 64 MiB of HBM per device.

v0:
```python
import jax
import jax.numpy as jnp
from jax import lax
from jax.sharding import PartitionSpec as P

DEGREE = 8
ITERS = 2
HALF_WIDTH = 2.0
EPSILON = 1e-06


def row_scaling(square_sums, live_counts, block):
    entries = (live_counts * block).astype(jnp.float32)[:, None]
    scaled = lax.rsqrt(square_sums / entries + EPSILON) / jnp.sqrt(entries)
    return (scaled / HALF_WIDTH).reshape(1, -1)


def chebyshev(first, apply):
    previous = first
    present = apply(first)
    for step in range(DEGREE - 1):
        previous, present = (present, 2.0 * apply(present) - previous)
    return present


def orthonormal(mine, total_rows):
    both = lax.all_gather(mine.astype(jnp.bfloat16), "vec", axis=0, tiled=True).astype(mine.dtype)
    part_gram = jnp.dot(both, both.T, precision=lax.Precision.HIGHEST)
    gram = lax.psum(part_gram, "row") / total_rows
    lower = jnp.linalg.cholesky(gram)
    solved = jax.scipy.linalg.solve_triangular(lower, both, lower=True)
    width = mine.shape[0]
    return lax.dynamic_slice_in_dim(solved, lax.axis_index("vec") * width, width, 0)


def per_device(start, tiles, pattern, counts):
    nb_dev = tiles.shape[0]
    block = tiles.shape[2]
    total_rows = nb_dev * block * lax.axis_size("row")
    vec_cols = start.shape[0]
    col_index = lax.axis_index("col")
    kb_dev = tiles.shape[1]
    slot_ids = col_index * kb_dev + jnp.arange(kb_dev, dtype=jnp.int32)
    live = (slot_ids[None, :] < counts[:, None]).astype(jnp.bfloat16)
    masked = tiles * live[:, :, None, None]
    local_pattern = lax.dynamic_slice_in_dim(pattern, col_index * kb_dev, kb_dev, 1)
    partial_squares = jnp.einsum(
        "bkmn,bkmn->bm", masked, masked, preferred_element_type=jnp.float32
    )
    square_sums = lax.psum(partial_squares, "col")
    scaling = row_scaling(square_sums, counts, block)

    def apply_slots(current):
        whole = lax.all_gather(current.astype(jnp.bfloat16), "row", axis=1, tiled=True)
        blocks = whole.reshape(vec_cols, -1, block)
        picked = jnp.take(blocks, local_pattern, axis=1)
        product = jnp.einsum("cbkn,bkmn->cbm", picked, masked, preferred_element_type=jnp.float32)
        total = lax.psum(product.astype(jnp.bfloat16), "col").astype(jnp.float32)
        return total.reshape(vec_cols, -1) * scaling

    current = start
    for outer in range(ITERS):
        filtered = chebyshev(current, apply_slots)
        current = orthonormal(filtered, total_rows)
    return current


def solution(mesh):
    in_specs = (
        P("vec", ("grp", "row")),
        P(("grp", "row"), "col", None, None),
        P(("grp", "row"), None),
        P(("grp", "row")),
    )
    out_specs = P("vec", ("grp", "row"))
    return jax.shard_map(
        per_device, mesh=mesh, in_specs=in_specs, out_specs=out_specs, check_vma=False
    )
```

profile of v0, /device:TPU:0, one launch (start us, length us, event | category | flops | bytes accessed | tf_op | source)
XLA Modules:
  0.0 427.7 jit_solution(17464882422868183498)
XLA Ops:
  0.0 0.8 compare_convert_fusion
  0.8 0.7 fusion.135
  1.5 0.7 multiply_convert_fusion
  2.2 1.6 fusion
  3.8 5.8 %psum.134 = f32[2,128]{1,0:T(2,128)S(1)} all-reduce(f32[2,128]{1,0:T(2,128)S(1)} %fusion), channel_id=1, replica_groups=mesh['grp'=2,'row'=4,'col'=2,'vec'=2] {'col'}, use_global_device_ids=true, to_apply=%region_1.0 | all-reduce | flops 256 | bytes 2048 | tf_op jit(solution)/shard_map/psum | solution.py:50
  9.9 14.0 %all_gather.54 = bf16[32,1024]{1,0:T(8,128)(2,1)S(1)} all-gather(bf16[32,256]{1,0:T(8,128)(2,1)S(1)} %convert_element_type.183), channel_id=1, replica_groups=mesh['grp'=2,'row'=4,'col'=2,'vec'=2] {'row'}, dimensions={1}, use_global_device_ids=true | all-gather | bytes 81920 | tf_op jit(solution)/shard_map/all_gather | solution.py:54
  23.9 0.6 gather_fusion
  25.1 8.2 %psum.133 = bf16[32,256]{1,0:T(8,128)(2,1)S(1)} all-reduce(bf16[32,256]{1,0:T(8,128)(2,1)S(1)} %bitcast.395), channel_id=1, replica_groups=mesh['grp'=2,'row'=4,'col'=2,'vec'=2] {'col'}, use_global_device_ids=true, to_apply=%region_0.2 | all-reduce | flops 8192 | bytes 32768 | tf_op jit(solution)/shard_map/psum | solution.py:58
  33.3 13.2 %all_gather.55 = bf16[32,1024]{1,0:T(8,128)(2,1)S(1)} all-gather(bf16[32,256]{1,0:T(8,128)(2,1)S(1)} %fusion.110), channel_id=1, replica_groups=mesh['grp'=2,'row'=4,'col'=2,'vec'=2] {'row'}, dimensions={1}, use_global_device_ids=true | all-gather | bytes 81920 | tf_op jit(solution)/shard_map/all_gather | solution.py:54
  46.5 0.6 gather_fusion.1
  47.6 7.2 %psum.135 = bf16[32,256]{1,0:T(8,128)(2,1)S(1)} all-reduce(bf16[32,256]{1,0:T(8,128)(2,1)S(1)} %bitcast.396), channel_id=1, replica_groups=mesh['grp'=2,'row'=4,'col'=2,'vec'=2] {'col'}, use_global_device_ids=true, to_apply=%region_2.4 | all-reduce | flops 8192 | bytes 32768 | tf_op jit(solution)/shard_map/psum | solution.py:58
  54.8 13.3 %all_gather.56 = bf16[32,1024]{1,0:T(8,128)(2,1)S(1)} all-gather(bf16[32,256]{1,0:T(8,128)(2,1)S(1)} %fusion.113), channel_id=1, replica_groups=mesh['grp'=2,'row'=4,'col'=2,'vec'=2] {'row'}, dimensions={1}, use_global_device_ids=true | all-gather | bytes 81920 | tf_op jit(solution)/shard_map/all_gather | solution.py:54
  68.1 0.6 gather_fusion.2
  69.2 8.1 %psum.136 = bf16[32,256]{1,0:T(8,128)(2,1)S(1)} all-reduce(bf16[32,256]{1,0:T(8,128)(2,1)S(1)} %bitcast.397), channel_id=1, replica_groups=mesh['grp'=2,'row'=4,'col'=2,'vec'=2] {'col'}, use_global_device_ids=true, to_apply=%region_3.5 | all-reduce | flops 8192 | bytes 32768 | tf_op jit(solution)/shard_map/psum | solution.py:58
  77.4 13.2 %all_gather.57 = bf16[32,1024]{1,0:T(8,128)(2,1)S(1)} all-gather(bf16[32,256]{1,0:T(8,128)(2,1)S(1)} %fusion.111), channel_id=1, replica_groups=mesh['grp'=2,'row'=4,'col'=2,'vec'=2] {'row'}, dimensions={1}, use_global_device_ids=true | all-gather | bytes 81920 | tf_op jit(solution)/shard_map/all_gather | solution.py:54
  90.6 0.6 gather_fusion.3
  91.7 7.2 %psum.137 = bf16[32,256]{1,0:T(8,128)(2,1)S(1)} all-reduce(bf16[32,256]{1,0:T(8,128)(2,1)S(1)} %bitcast.398), channel_id=1, replica_groups=mesh['grp'=2,'row'=4,'col'=2,'vec'=2] {'col'}, use_global_device_ids=true, to_apply=%region_4.6 | all-reduce | flops 8192 | bytes 32768 | tf_op jit(solution)/shard_map/psum | solution.py:58
  98.9 13.2 %all_gather.58 = bf16[32,1024]{1,0:T(8,128)(2,1)S(1)} all-gather(bf16[32,256]{1,0:T(8,128)(2,1)S(1)} %fusion.137), channel_id=1, replica_groups=mesh['grp'=2,'row'=4,'col'=2,'vec'=2] {'row'}, dimensions={1}, use_global_device_ids=true | all-gather | bytes 81920 | tf_op jit(solution)/shard_map/all_gather | solution.py:54
  112.1 0.6 gather_fusion.4
  113.3 8.1 %psum.138 = bf16[32,256]{1,0:T(8,128)(2,1)S(1)} all-reduce(bf16[32,256]{1,0:T(8,128)(2,1)S(1)} %bitcast.399), channel_id=1, replica_groups=mesh['grp'=2,'row'=4,'col'=2,'vec'=2] {'col'}, use_global_device_ids=true, to_apply=%region_5.7 | all-reduce | flops 8192 | bytes 32768 | tf_op jit(solution)/shard_map/psum | solution.py:58
  121.5 13.1 %all_gather.59 = bf16[32,1024]{1,0:T(8,128)(2,1)S(1)} all-gather(bf16[32,256]{1,0:T(8,128)(2,1)S(1)} %fusion.116), channel_id=1, replica_groups=mesh['grp'=2,'row'=4,'col'=2,'vec'=2] {'row'}, dimensions={1}, use_global_device_ids=true | all-gather | bytes 81920 | tf_op jit(solution)/shard_map/all_gather | solution.py:54
  134.6 0.6 gather_fusion.5
  135.8 7.3 %psum.139 = bf16[32,256]{1,0:T(8,128)(2,1)S(1)} all-reduce(bf16[32,256]{1,0:T(8,128)(2,1)S(1)} %bitcast.400), channel_id=1, replica_groups=mesh['grp'=2,'row'=4,'col'=2,'vec'=2] {'col'}, use_global_device_ids=true, to_apply=%region_6.8 | all-reduce | flops 8192 | bytes 32768 | tf_op jit(solution)/shard_map/psum | solution.py:58
  143.1 13.2 %all_gather.60 = bf16[32,1024]{1,0:T(8,128)(2,1)S(1)} all-gather(bf16[32,256]{1,0:T(8,128)(2,1)S(1)} %fusion.114), channel_id=1, replica_groups=mesh['grp'=2,'row'=4,'col'=2,'vec'=2] {'row'}, dimensions={1}, use_global_device_ids=true | all-gather | bytes 81920 | tf_op jit(solution)/shard_map/all_gather | solution.py:54
  156.3 0.6 gather_fusion.6
  157.4 8.0 %psum.140 = bf16[32,256]{1,0:T(8,128)(2,1)S(1)} all-reduce(bf16[32,256]{1,0:T(8,128)(2,1)S(1)} %bitcast.401), channel_id=1, replica_groups=mesh['grp'=2,'row'=4,'col'=2,'vec'=2] {'col'}, use_global_device_ids=true, to_apply=%region_7.9 | all-reduce | flops 8192 | bytes 32768 | tf_op jit(solution)/shard_map/psum | solution.py:58
  165.5 13.1 %all_gather.61 = bf16[32,1024]{1,0:T(8,128)(2,1)S(1)} all-gather(bf16[32,256]{1,0:T(8,128)(2,1)S(1)} %subtract_convert_fusion.3), channel_id=1, replica_groups=mesh['grp'=2,'row'=4,'col'=2,'vec'=2] {'row'}, dimensions={1}, use_global_device_ids=true | all-gather | bytes 81920 | tf_op jit(solution)/shard_map/all_gather | solution.py:54
  178.6 0.6 gather_fusion.7
  179.8 7.3 %psum.141 = bf16[32,256]{1,0:T(8,128)(2,1)S(1)} all-reduce(bf16[32,256]{1,0:T(8,128)(2,1)S(1)} %bitcast.402), channel_id=1, replica_groups=mesh['grp'=2,'row'=4,'col'=2,'vec'=2] {'col'}, use_global_device_ids=true, to_apply=%region_8.10 | all-reduce | flops 8192 | bytes 32768 | tf_op jit(solution)/shard_map/psum | solution.py:58
  187.1 1.8 all_gather.62
  189.1 18.8 %psum.142 = f32[64,64]{0,1:T(8,128)S(1)} all-reduce(f32[64,64]{0,1:T(8,128)S(1)} %fusion.138), channel_id=1, replica_groups=mesh['grp'=2,'row'=4,'col'=2,'vec'=2] {'row'}, use_global_device_ids=true, to_apply=%region_9.11 | all-reduce | flops 4096 | bytes 32768 | tf_op jit(solution)/shard_map/psum | solution.py:29
  208.1 5.8 %cholesky.44 = f32[64,64]{1,0:T(8,128)S(1)} custom-call(f32[64,64]{1,0:T(8,128)S(1)} %fusion.106), custom_call_target="Cholesky" | custom-call | tf_op jit(solution)/shard_map/jit(cholesky)/cholesky | solution.py:30
  213.9 0.6 compare_reduce_fusion.1
  214.6 0.7 fusion.101
  215.2 4.9 %custom-call.6 = f32[1,64,64]{1,2,0:T(8,128)S(1)} custom-call(f32[1,64,64]{2,1,0:T(8,128)S(1)} %fusion.101), custom_call_target="InvertDiagBlocksLowerTriangular" | custom-call | tf_op jit(solution)/shard_map/jit(_solve_triangular)/triangular_solve | solution.py:31
  220.4 13.1 %all_gather.63 = bf16[32,1024]{1,0:T(8,128)(2,1)S(1)} all-gather(bf16[32,256]{1,0:T(8,128)(2,1)S(1)} %dynamic-slice_convert_fusion), channel_id=1, replica_groups=mesh['grp'=2,'row'=4,'col'=2,'vec'=2] {'row'}, dimensions={1}, use_global_device_ids=true | all-gather | bytes 81920 | tf_op jit(solution)/shard_map/all_gather | solution.py:54
  233.6 0.6 gather_fusion.8
  234.7 8.0 %psum.143 = bf16[32,256]{1,0:T(8,128)(2,1)S(1)} all-reduce(bf16[32,256]{1,0:T(8,128)(2,1)S(1)} %bitcast.403), channel_id=1, replica_groups=mesh['grp'=2,'row'=4,'col'=2,'vec'=2] {'col'}, use_global_device_ids=true, to_apply=%region_12.16 | all-reduce | flops 8192 | bytes 32768 | tf_op jit(solution)/shard_map/psum | solution.py:58
  242.8 13.2 %all_gather.64 = bf16[32,1024]{1,0:T(8,128)(2,1)S(1)} all-gather(bf16[32,256]{1,0:T(8,128)(2,1)S(1)} %fusion.109), channel_id=1, replica_groups=mesh['grp'=2,'row'=4,'col'=2,'vec'=2] {'row'}, dimensions={1}, use_global_device_ids=true | all-gather | bytes 81920 | tf_op jit(solution)/shard_map/all_gather | solution.py:54
  256.0 0.6 gather_fusion.9
  257.1 7.3 %psum.144 = bf16[32,256]{1,0:T(8,128)(2,1)S(1)} all-reduce(bf16[32,256]{1,0:T(8,128)(2,1)S(1)} %bitcast.404), channel_id=1, replica_groups=mesh['grp'=2,'row'=4,'col'=2,'vec'=2] {'col'}, use_global_device_ids=true, to_apply=%region_13.17 | all-reduce | flops 8192 | bytes 32768 | tf_op jit(solution)/shard_map/psum | solution.py:58
  264.4 13.1 %all_gather.65 = bf16[32,1024]{1,0:T(8,128)(2,1)S(1)} all-gather(bf16[32,256]{1,0:T(8,128)(2,1)S(1)} %fusion.136), channel_id=1, replica_groups=mesh['grp'=2,'row'=4,'col'=2,'vec'=2] {'row'}, dimensions={1}, use_global_device_ids=true | all-gather | bytes 81920 | tf_op jit(solution)/shard_map/all_gather | solution.py:54
  277.6 0.6 gather_fusion.10
  278.8 8.0 %psum.145 = bf16[32,256]{1,0:T(8,128)(2,1)S(1)} all-reduce(bf16[32,256]{1,0:T(8,128)(2,1)S(1)} %bitcast.405), channel_id=1, replica_groups=mesh['grp'=2,'row'=4,'col'=2,'vec'=2] {'col'}, use_global_device_ids=true, to_apply=%region_14.18 | all-reduce | flops 8192 | bytes 32768 | tf_op jit(solution)/shard_map/psum | solution.py:58
  286.8 13.1 %all_gather.66 = bf16[32,1024]{1,0:T(8,128)(2,1)S(1)} all-gather(bf16[32,256]{1,0:T(8,128)(2,1)S(1)} %fusion.112), channel_id=1, replica_groups=mesh['grp'=2,'row'=4,'col'=2,'vec'=2] {'row'}, dimensions={1}, use_global_device_ids=true | all-gather | bytes 81920 | tf_op jit(solution)/shard_map/all_gather | solution.py:54
  300.0 0.6 gather_fusion.11
  301.1 7.3 %psum.146 = bf16[32,256]{1,0:T(8,128)(2,1)S(1)} all-reduce(bf16[32,256]{1,0:T(8,128)(2,1)S(1)} %bitcast.406), channel_id=1, replica_groups=mesh['grp'=2,'row'=4,'col'=2,'vec'=2] {'col'}, use_global_device_ids=true, to_apply=%region_15.19 | all-reduce | flops 8192 | bytes 32768 | tf_op jit(solution)/shard_map/psum | solution.py:58
  308.5 13.2 %all_gather.67 = bf16[32,1024]{1,0:T(8,128)(2,1)S(1)} all-gather(bf16[32,256]{1,0:T(8,128)(2,1)S(1)} %fusion.115), channel_id=1, replica_groups=mesh['grp'=2,'row'=4,'col'=2,'vec'=2] {'row'}, dimensions={1}, use_global_device_ids=true | all-gather | bytes 81920 | tf_op jit(solution)/shard_map/all_gather | solution.py:54
  321.7 0.6 gather_fusion.12
  322.8 8.0 %psum.147 = bf16[32,256]{1,0:T(8,128)(2,1)S(1)} all-reduce(bf16[32,256]{1,0:T(8,128)(2,1)S(1)} %bitcast.407), channel_id=1, replica_groups=mesh['grp'=2,'row'=4,'col'=2,'vec'=2] {'col'}, use_global_device_ids=true, to_apply=%region_16.20 | all-reduce | flops 8192 | bytes 32768 | tf_op jit(solution)/shard_map/psum | solution.py:58
  330.8 13.3 %all_gather.68 = bf16[32,1024]{1,0:T(8,128)(2,1)S(1)} all-gather(bf16[32,256]{1,0:T(8,128)(2,1)S(1)} %fusion.117), channel_id=1, replica_groups=mesh['grp'=2,'row'=4,'col'=2,'vec'=2] {'row'}, dimensions={1}, use_global_device_ids=true | all-gather | bytes 81920 | tf_op jit(solution)/shard_map/all_gather | solution.py:54
  344.2 0.6 gather_fusion.13
  345.3 7.4 %psum.148 = bf16[32,256]{1,0:T(8,128)(2,1)S(1)} all-reduce(bf16[32,256]{1,0:T(8,128)(2,1)S(1)} %bitcast.408), channel_id=1, replica_groups=mesh['grp'=2,'row'=4,'col'=2,'vec'=2] {'col'}, use_global_device_ids=true, to_apply=%region_17.21 | all-reduce | flops 8192 | bytes 32768 | tf_op jit(solution)/shard_map/psum | solution.py:58
  352.7 13.1 %all_gather.69 = bf16[32,1024]{1,0:T(8,128)(2,1)S(1)} all-gather(bf16[32,256]{1,0:T(8,128)(2,1)S(1)} %fusion.118), channel_id=1, replica_groups=mesh['grp'=2,'row'=4,'col'=2,'vec'=2] {'row'}, dimensions={1}, use_global_device_ids=true | all-gather | bytes 81920 | tf_op jit(solution)/shard_map/all_gather | solution.py:54
  367.0 8.0 %psum.149 = bf16[32,256]{1,0:T(8,128)(2,1)S(1)} all-reduce(bf16[32,256]{1,0:T(8,128)(2,1)S(1)} %bitcast.409), channel_id=1, replica_groups=mesh['grp'=2,'row'=4,'col'=2,'vec'=2] {'col'}, use_global_device_ids=true, to_apply=%region_18.22 | all-reduce | flops 8192 | bytes 32768 | tf_op jit(solution)/shard_map/psum | solution.py:58
  375.0 13.1 %all_gather.70 = bf16[32,1024]{1,0:T(8,128)(2,1)S(1)} all-gather(bf16[32,256]{1,0:T(8,128)(2,1)S(1)} %subtract_convert_fusion.1), channel_id=1, replica_groups=mesh['grp'=2,'row'=4,'col'=2,'vec'=2] {'row'}, dimensions={1}, use_global_device_ids=true | all-gather | bytes 81920 | tf_op jit(solution)/shard_map/all_gather | solution.py:54
  389.3 7.4 %psum.150 = bf16[32,256]{1,0:T(8,128)(2,1)S(1)} all-reduce(bf16[32,256]{1,0:T(8,128)(2,1)S(1)} %bitcast.410), channel_id=1, replica_groups=mesh['grp'=2,'row'=4,'col'=2,'vec'=2] {'col'}, use_global_device_ids=true, to_apply=%region_19.23 | all-reduce | flops 8192 | bytes 32768 | tf_op jit(solution)/shard_map/psum | solution.py:58
  396.8 1.8 all_gather.71
  398.7 15.9 %psum.151 = f32[64,64]{0,1:T(8,128)S(1)} all-reduce(f32[64,64]{0,1:T(8,128)S(1)} %fusion.139), channel_id=1, replica_groups=mesh['grp'=2,'row'=4,'col'=2,'vec'=2] {'row'}, use_global_device_ids=true, to_apply=%region_20.24 | all-reduce | flops 4096 | bytes 32768 | tf_op jit(solution)/shard_map/psum | solution.py:29
  414.7 5.8 %cholesky.55 = f32[64,64]{1,0:T(8,128)S(1)} custom-call(f32[64,64]{1,0:T(8,128)S(1)} %fusion.104), custom_call_target="Cholesky" | custom-call | tf_op jit(solution)/shard_map/jit(cholesky)/cholesky | solution.py:30
  420.6 0.6 compare_reduce_fusion
  421.3 0.7 fusion.102
  421.9 4.9 %custom-call.7 = f32[1,64,64]{1,2,0:T(8,128)S(1)} custom-call(f32[1,64,64]{2,1,0:T(8,128)S(1)} %fusion.102), custom_call_target="InvertDiagBlocksLowerTriangular" | custom-call | tf_op jit(solution)/shard_map/jit(_solve_triangular)/triangular_solve | solution.py:31
  427.1 0.6 constant_dynamic-slice_fusion
  (91 shorter events, 11.5 us)
Async XLA Ops:
  0.0 24.5 %copy-start = (bf16[2,16,128,128]{3,2,1,0:T(8,128)(2,1)S(1)}, bf16[2,16,128,128]{3,2,1,0:T(8,128)(2,1)}, u32[]{:S(2)}) copy-start(bf16[2,16,128,128]{3,2,1,0:T(8,128)(2,1)} %param.10) | copy-start | bytes 3145732
  0.0 9.9 %copy-start.1 = (f32[32,256]{1,0:T(8,128)S(1)}, f32[32,256]{1,0:T(8,128)}, u32[]{:S(2)}) copy-start(f32[32,256]{1,0:T(8,128)} %param.9) | copy-start | bytes 98308
  0.0 9.7 %copy-start.2 = (s32[2,32]{1,0:T(2,128)S(1)}, s32[2,32]{1,0:T(2,128)}, u32[]{:S(2)}) copy-start(s32[2,32]{1,0:T(2,128)} %param.11) | copy-start | bytes 772
where the time goes:
time: 429 us; the launch traced here: 428 us
  blocking collectives  379 us (88%)
  other arithmetic  28.4 us (7%)
  local copies, waits for them, and re-layouts  11 us (3%)
  matrix products  9.04 us (2%)
    all_gather x16, blocking collectives, apply_slots(): lax.all_gather(current.astype(jnp.bfloat16), 'row', axis=1, tiled=True)  212 us
    psum x16, blocking collectives, apply_slots(): total = lax.psum(product.astype(jnp.bfloat16), 'col').astype(jnp.float32)  123 us
    psum x2, blocking collectives, orthonormal(): gram = lax.psum(part_gram, 'row') / total_rows  34.8 us
    another operation x6, other arithmetic, orthonormal(): lower = jnp.linalg.cholesky(gram)  13 us
    another operation x4, other arithmetic, orthonormal(): solved = jax.scipy.linalg.solve_triangular(lower, both, lower=True)  11.1 us
    gather x16, local copies, waits for them, and re-layouts, apply_slots(): picked = jnp.take(blocks, local_pattern, axis=1)  9.63 us

commit v1 on v0

--- a/solution.py
+++ b/solution.py
@@ -7,6 +7,28 @@
 ITERS = 2
 HALF_WIDTH = 2.0
 EPSILON = 1e-06
+
+
+def joined_along(tiles, dim):
+    shape = list(tiles.shape[1:])
+    shape[dim] *= tiles.shape[0]
+    return jnp.moveaxis(tiles, 0, dim).reshape(shape)
+
+
+def collect(x, axis, dim):
+    size = lax.axis_size(axis)
+    pairs = [(i, (i + 1) % size) for i in range(size)]
+    back = [(b, a) for a, b in pairs]
+    lower, upper = ([], [])
+    for lap in range(size - 1):
+        if lap % 2 == 0:
+            lower.append(lax.ppermute(lower[-1] if lower else x, axis, pairs))
+        else:
+            upper.append(lax.ppermute(upper[-1] if upper else x, axis, back))
+    blocks = jnp.stack([*lower[::-1], x, *upper])
+    shift = lax.axis_index(axis) - len(lower)
+    blocks = blocks[(jnp.arange(size) - shift) % size]
+    return joined_along(blocks, dim)
 
 
 def row_scaling(square_sums, live_counts, block):
@@ -51,7 +73,7 @@
     scaling = row_scaling(square_sums, counts, block)
 
     def apply_slots(current):
-        whole = lax.all_gather(current.astype(jnp.bfloat16), "row", axis=1, tiled=True)
+        whole = collect(current.astype(jnp.bfloat16), "row", 1)
         blocks = whole.reshape(vec_cols, -1, block)
         picked = jnp.take(blocks, local_pattern, axis=1)
         product = jnp.einsum("cbkn,bkmn->cbm", picked, masked, preferred_element_type=jnp.float32)

time: 429 us -> 403 us (0.939)
  blocking collectives: 379 us -> 163 us
  waiting for transfers between devices: 0 us -> 113 us
  starting transfers between devices: 0 us -> 63.5 us
  local copies, waits for them, and re-layouts: 11 us -> 21.4 us
    all_gather x16 -> x0, blocking collectives: 212 us -> none  [apply_slots(): lax.all_gather(current.astype(jnp.bfloat16), 'row', axis=1, tiled=True)]
    ppermute x0 -> x48, waiting for transfers between devices: none -> 113 us  [the longest x32 113 us: collect(): lower.append(lax.ppermute(lower[-1] if lower else x, axis, pairs))]
    ppermute x0 -> x48, starting transfers between devices: none -> 63.5 us  [the longest x16 62.3 us: collect(): upper.append(lax.ppermute(upper[-1] if upper else x, axis, back))]
    gather x0 -> x16, local copies, waits for them, and re-layouts: none -> 8.82 us  [collect(): blocks = blocks[(jnp.arange(size) - shift) % size]]
  transfers between devices with their start and end apart: 0 -> 48, of which waited for: 0 -> 31; matrix products, arithmetic and copies ran while one was open for 0% -> 1% of each run, Pallas kernels for 0% -> 0%
where the time goes in v1:
time: 403 us; the launch traced here: 402 us
  blocking collectives  163 us (40%)
  waiting for transfers between devices  113 us (28%)
  starting transfers between devices  63.5 us (16%)
  other arithmetic  30.2 us (7%)
  local copies, waits for them, and re-layouts  21.4 us (5%)
  matrix products  9.03 us (2%)
    psum x16, blocking collectives, apply_slots(): total = lax.psum(product.astype(jnp.bfloat16), 'col').astype(jnp.float32)  123 us
    ppermute x32, waiting for transfers between devices, collect(): lower.append(lax.ppermute(lower[-1] if lower else x, axis, pairs))  113 us
    ppermute x16, starting transfers between devices, collect(): upper.append(lax.ppermute(upper[-1] if upper else x, axis, back))  62.3 us
    psum x2, blocking collectives, orthonormal(): gram = lax.psum(part_gram, 'row') / total_rows  31.5 us
    another operation x6, other arithmetic, orthonormal(): lower = jnp.linalg.cholesky(gram)  13 us
    another operation x4, other arithmetic, orthonormal(): solved = jax.scipy.linalg.solve_triangular(lower, both, lower=True)  11.1 us
    gather x16, local copies, waits for them, and re-layouts, apply_slots(): picked = jnp.take(blocks, local_pattern, axis=1)  9.63 us
    gather x16, local copies, waits for them, and re-layouts, collect(): blocks = blocks[(jnp.arange(size) - shift) % size]  8.82 us
  transfers between devices with their start and end apart: 48, of which 31 were waited for; matrix products, arithmetic and copies ran while one was open for 1% of the time, Pallas kernels for 0%

profile of v1, /device:TPU:0, one launch (start us, length us, event | category | flops | bytes accessed | tf_op | source)
XLA Modules:
  0.0 401.8 jit_solution(5434419362011797606)
XLA Ops:
  0.8 5.0 %collective-permute-start.2 = (bf16[32,256]{1,0:T(8,128)(2,1)S(1)}, bf16[32,256]{1,0:T(8,128)(2,1)S(1)}, u32[]{:S(2)}, u32[]{:S(2)}) collective-permute-start(bf16[32,256]{1,0:T(8,128)(2,1)S(1)} %convert_element_type.271), channel_id=1, source_target_pairs={{4,0},{8,4},{12,8},{0,12},{5,1},{9,5},{13,9},{1,13},{6,2},{10,6},{... | collective-permute-start | bytes 49160 | tf_op jit(solution)/shard_map/ppermute | solution.py:27
  8.6 1.7 fusion
  10.4 4.9 %psum.134 = f32[2,128]{1,0:T(2,128)S(1)} all-reduce(f32[2,128]{1,0:T(2,128)S(1)} %fusion), channel_id=1, replica_groups=mesh['grp'=2,'row'=4,'col'=2,'vec'=2] {'col'}, use_global_device_ids=true, to_apply=%region_1.3 | all-reduce | flops 256 | bytes 2048 | tf_op jit(solution)/shard_map/psum | solution.py:72
  15.7 5.5 %collective-permute-done.1 = bf16[32,256]{1,0:T(8,128)(2,1)S(1)} collective-permute-done((bf16[32,256]{1,0:T(8,128)(2,1)S(1)}, bf16[32,256]{1,0:T(8,128)(2,1)S(1)}, u32[]{:S(2)}, u32[]{:S(2)}) %collective-permute-start.1) | collective-permute-done | bytes 16416 | tf_op jit(solution)/shard_map/ppermute | solution.py:25
  23.0 8.2 %psum.133 = bf16[32,2,128]{2,0,1:T(8,128)(2,1)S(1)} all-reduce(bf16[32,2,128]{2,0,1:T(8,128)(2,1)S(1)} %fusion.32), channel_id=1, replica_groups=mesh['grp'=2,'row'=4,'col'=2,'vec'=2] {'col'}, use_global_device_ids=true, to_apply=%region_0.2 | all-reduce | flops 8192 | bytes 32768 | tf_op jit(solution)/shard_map/psum | solution.py:80
  31.3 3.8 collective-permute-start.5
  36.8 5.5 %collective-permute-done.4 = bf16[32,256]{1,0:T(8,128)(2,1)S(1)} collective-permute-done((bf16[32,256]{1,0:T(8,128)(2,1)S(1)}, bf16[32,256]{1,0:T(8,128)(2,1)S(1)}, u32[]{:S(2)}, u32[]{:S(2)}) %collective-permute-start.4) | collective-permute-done | bytes 16416 | tf_op jit(solution)/shard_map/ppermute | solution.py:25
  44.2 7.2 %psum.135 = bf16[32,256]{1,0:T(8,128)(2,1)S(1)} all-reduce(bf16[32,256]{1,0:T(8,128)(2,1)S(1)} %bitcast.495), channel_id=1, replica_groups=mesh['grp'=2,'row'=4,'col'=2,'vec'=2] {'col'}, use_global_device_ids=true, to_apply=%region_2.4 | all-reduce | flops 8192 | bytes 32768 | tf_op jit(solution)/shard_map/psum | solution.py:80
  51.5 3.8 collective-permute-start.8
  55.3 1.7 collective-permute-done.6
  57.0 5.5 %collective-permute-done.7 = bf16[32,256]{1,0:T(8,128)(2,1)S(1)} collective-permute-done((bf16[32,256]{1,0:T(8,128)(2,1)S(1)}, bf16[32,256]{1,0:T(8,128)(2,1)S(1)}, u32[]{:S(2)}, u32[]{:S(2)}) %collective-permute-start.7) | collective-permute-done | bytes 16416 | tf_op jit(solution)/shard_map/ppermute | solution.py:25
  64.3 8.2 %psum.136 = bf16[32,2,128]{2,0,1:T(8,128)(2,1)S(1)} all-reduce(bf16[32,2,128]{2,0,1:T(8,128)(2,1)S(1)} %fusion.30), channel_id=1, replica_groups=mesh['grp'=2,'row'=4,'col'=2,'vec'=2] {'col'}, use_global_device_ids=true, to_apply=%region_3.5 | all-reduce | flops 8192 | bytes 32768 | tf_op jit(solution)/shard_map/psum | solution.py:80
  72.6 3.8 collective-permute-start.11
  78.1 5.5 %collective-permute-done.10 = bf16[32,256]{1,0:T(8,128)(2,1)S(1)} collective-permute-done((bf16[32,256]{1,0:T(8,128)(2,1)S(1)}, bf16[32,256]{1,0:T(8,128)(2,1)S(1)}, u32[]{:S(2)}, u32[]{:S(2)}) %collective-permute-start.10) | collective-permute-done | bytes 16416 | tf_op jit(solution)/shard_map/ppermute | solution.py:25
  85.5 7.2 %psum.137 = bf16[32,256]{1,0:T(8,128)(2,1)S(1)} all-reduce(bf16[32,256]{1,0:T(8,128)(2,1)S(1)} %bitcast.496), channel_id=1, replica_groups=mesh['grp'=2,'row'=4,'col'=2,'vec'=2] {'col'}, use_global_device_ids=true, to_apply=%region_4.6 | all-reduce | flops 8192 | bytes 32768 | tf_op jit(solution)/shard_map/psum | solution.py:80
  92.8 3.8 collective-permute-start.14
  96.6 1.7 collective-permute-done.12
  98.3 5.5 %collective-permute-done.13 = bf16[32,256]{1,0:T(8,128)(2,1)S(1)} collective-permute-done((bf16[32,256]{1,0:T(8,128)(2,1)S(1)}, bf16[32,256]{1,0:T(8,128)(2,1)S(1)}, u32[]{:S(2)}, u32[]{:S(2)}) %collective-permute-start.13) | collective-permute-done | bytes 16416 | tf_op jit(solution)/shard_map/ppermute | solution.py:25
  105.6 8.2 %psum.138 = bf16[32,2,128]{2,0,1:T(8,128)(2,1)S(1)} all-reduce(bf16[32,2,128]{2,0,1:T(8,128)(2,1)S(1)} %fusion.28), channel_id=1, replica_groups=mesh['grp'=2,'row'=4,'col'=2,'vec'=2] {'col'}, use_global_device_ids=true, to_apply=%region_5.7 | all-reduce | flops 8192 | bytes 32768 | tf_op jit(solution)/shard_map/psum | solution.py:80
  113.9 3.8 collective-permute-start.17
  119.5 5.5 %collective-permute-done.16 = bf16[32,256]{1,0:T(8,128)(2,1)S(1)} collective-permute-done((bf16[32,256]{1,0:T(8,128)(2,1)S(1)}, bf16[32,256]{1,0:T(8,128)(2,1)S(1)}, u32[]{:S(2)}, u32[]{:S(2)}) %collective-permute-start.16) | collective-permute-done | bytes 16416 | tf_op jit(solution)/shard_map/ppermute | solution.py:25
  126.8 7.2 %psum.139 = bf16[32,256]{1,0:T(8,128)(2,1)S(1)} all-reduce(bf16[32,256]{1,0:T(8,128)(2,1)S(1)} %bitcast.497), channel_id=1, replica_groups=mesh['grp'=2,'row'=4,'col'=2,'vec'=2] {'col'}, use_global_device_ids=true, to_apply=%region_6.8 | all-reduce | flops 8192 | bytes 32768 | tf_op jit(solution)/shard_map/psum | solution.py:80
  134.1 3.8 collective-permute-start.20
  137.9 1.7 collective-permute-done.18
  139.6 5.5 %collective-permute-done.19 = bf16[32,256]{1,0:T(8,128)(2,1)S(1)} collective-permute-done((bf16[32,256]{1,0:T(8,128)(2,1)S(1)}, bf16[32,256]{1,0:T(8,128)(2,1)S(1)}, u32[]{:S(2)}, u32[]{:S(2)}) %collective-permute-start.19) | collective-permute-done | bytes 16416 | tf_op jit(solution)/shard_map/ppermute | solution.py:25
  147.0 8.2 %psum.140 = bf16[32,2,128]{2,0,1:T(8,128)(2,1)S(1)} all-reduce(bf16[32,2,128]{2,0,1:T(8,128)(2,1)S(1)} %fusion.26), channel_id=1, replica_groups=mesh['grp'=2,'row'=4,'col'=2,'vec'=2] {'col'}, use_global_device_ids=true, to_apply=%region_7.9 | all-reduce | flops 8192 | bytes 32768 | tf_op jit(solution)/shard_map/psum | solution.py:80
  155.3 3.9 collective-permute-start.23
  160.8 5.5 %collective-permute-done.22 = bf16[32,256]{1,0:T(8,128)(2,1)S(1)} collective-permute-done((bf16[32,256]{1,0:T(8,128)(2,1)S(1)}, bf16[32,256]{1,0:T(8,128)(2,1)S(1)}, u32[]{:S(2)}, u32[]{:S(2)}) %collective-permute-start.22) | collective-permute-done | bytes 16416 | tf_op jit(solution)/shard_map/ppermute | solution.py:25
  168.2 7.2 %psum.141 = bf16[32,256]{1,0:T(8,128)(2,1)S(1)} all-reduce(bf16[32,256]{1,0:T(8,128)(2,1)S(1)} %bitcast.498), channel_id=1, replica_groups=mesh['grp'=2,'row'=4,'col'=2,'vec'=2] {'col'}, use_global_device_ids=true, to_apply=%region_8.10 | all-reduce | flops 8192 | bytes 32768 | tf_op jit(solution)/shard_map/psum | solution.py:80
  175.4 1.8 all_gather.6
  177.3 15.8 %psum.142 = f32[64,64]{0,1:T(8,128)S(1)} all-reduce(f32[64,64]{0,1:T(8,128)S(1)} %fusion.158), channel_id=1, replica_groups=mesh['grp'=2,'row'=4,'col'=2,'vec'=2] {'row'}, use_global_device_ids=true, to_apply=%region_9.11 | all-reduce | flops 4096 | bytes 32768 | tf_op jit(solution)/shard_map/psum | solution.py:51
  193.2 5.8 %cholesky.44 = f32[64,64]{1,0:T(8,128)S(1)} custom-call(f32[64,64]{1,0:T(8,128)S(1)} %fusion.120), custom_call_target="Cholesky" | custom-call | tf_op jit(solution)/shard_map/jit(cholesky)/cholesky | solution.py:52
  200.4 4.9 %custom-call.6 = f32[1,64,64]{1,2,0:T(8,128)S(1)} custom-call(f32[1,64,64]{2,1,0:T(8,128)S(1)} %fusion.101), custom_call_target="InvertDiagBlocksLowerTriangular" | custom-call | tf_op jit(solution)/shard_map/jit(_solve_triangular)/triangular_solve | solution.py:53
  205.7 3.8 collective-permute-start.26
  209.5 1.7 collective-permute-done.24
  211.2 5.5 %collective-permute-done.25 = bf16[32,256]{1,0:T(8,128)(2,1)S(1)} collective-permute-done((bf16[32,256]{1,0:T(8,128)(2,1)S(1)}, bf16[32,256]{1,0:T(8,128)(2,1)S(1)}, u32[]{:S(2)}, u32[]{:S(2)}) %collective-permute-start.25) | collective-permute-done | bytes 16416 | tf_op jit(solution)/shard_map/ppermute | solution.py:25
  218.5 8.2 %psum.143 = bf16[32,2,128]{2,0,1:T(8,128)(2,1)S(1)} all-reduce(bf16[32,2,128]{2,0,1:T(8,128)(2,1)S(1)} %fusion.24), channel_id=1, replica_groups=mesh['grp'=2,'row'=4,'col'=2,'vec'=2] {'col'}, use_global_device_ids=true, to_apply=%region_12.16 | all-reduce | flops 8192 | bytes 32768 | tf_op jit(solution)/shard_map/psum | solution.py:80
  227.0 3.8 collective-permute-start.29
  232.5 5.5 %collective-permute-done.28 = bf16[32,256]{1,0:T(8,128)(2,1)S(1)} collective-permute-done((bf16[32,256]{1,0:T(8,128)(2,1)S(1)}, bf16[32,256]{1,0:T(8,128)(2,1)S(1)}, u32[]{:S(2)}, u32[]{:S(2)}) %collective-permute-start.28) | collective-permute-done | bytes 16416 | tf_op jit(solution)/shard_map/ppermute | solution.py:25
  239.9 7.2 %psum.144 = bf16[32,256]{1,0:T(8,128)(2,1)S(1)} all-reduce(bf16[32,256]{1,0:T(8,128)(2,1)S(1)} %bitcast.499), channel_id=1, replica_groups=mesh['grp'=2,'row'=4,'col'=2,'vec'=2] {'col'}, use_global_device_ids=true, to_apply=%region_13.17 | all-reduce | flops 8192 | bytes 32768 | tf_op jit(solution)/shard_map/psum | solution.py:80
  247.1 3.8 collective-permute-start.32
  250.9 1.7 collective-permute-done.30
  252.6 5.5 %collective-permute-done.31 = bf16[32,256]{1,0:T(8,128)(2,1)S(1)} collective-permute-done((bf16[32,256]{1,0:T(8,128)(2,1)S(1)}, bf16[32,256]{1,0:T(8,128)(2,1)S(1)}, u32[]{:S(2)}, u32[]{:S(2)}) %collective-permute-start.31) | collective-permute-done | bytes 16416 | tf_op jit(solution)/shard_map/ppermute | solution.py:25
  260.0 8.3 %psum.145 = bf16[32,2,128]{2,0,1:T(8,128)(2,1)S(1)} all-reduce(bf16[32,2,128]{2,0,1:T(8,128)(2,1)S(1)} %fusion.22), channel_id=1, replica_groups=mesh['grp'=2,'row'=4,'col'=2,'vec'=2] {'col'}, use_global_device_ids=true, to_apply=%region_14.18 | all-reduce | flops 8192 | bytes 32768 | tf_op jit(solution)/shard_map/psum | solution.py:80
  268.4 3.8 collective-permute-start.35
  273.9 5.5 %collective-permute-done.34 = bf16[32,256]{1,0:T(8,128)(2,1)S(1)} collective-permute-done((bf16[32,256]{1,0:T(8,128)(2,1)S(1)}, bf16[32,256]{1,0:T(8,128)(2,1)S(1)}, u32[]{:S(2)}, u32[]{:S(2)}) %collective-permute-start.34) | collective-permute-done | bytes 16416 | tf_op jit(solution)/shard_map/ppermute | solution.py:25
  281.3 7.1 %psum.146 = bf16[32,256]{1,0:T(8,128)(2,1)S(1)} all-reduce(bf16[32,256]{1,0:T(8,128)(2,1)S(1)} %bitcast.500), channel_id=1, replica_groups=mesh['grp'=2,'row'=4,'col'=2,'vec'=2] {'col'}, use_global_device_ids=true, to_apply=%region_15.19 | all-reduce | flops 8192 | bytes 32768 | tf_op jit(solution)/shard_map/psum | solution.py:80
  288.4 3.8 collective-permute-start.38
  292.2 1.7 collective-permute-done.36
  294.0 5.5 %collective-permute-done.37 = bf16[32,256]{1,0:T(8,128)(2,1)S(1)} collective-permute-done((bf16[32,256]{1,0:T(8,128)(2,1)S(1)}, bf16[32,256]{1,0:T(8,128)(2,1)S(1)}, u32[]{:S(2)}, u32[]{:S(2)}) %collective-permute-start.37) | collective-permute-done | bytes 16416 | tf_op jit(solution)/shard_map/ppermute | solution.py:25
  301.3 8.3 %psum.147 = bf16[32,2,128]{2,0,1:T(8,128)(2,1)S(1)} all-reduce(bf16[32,2,128]{2,0,1:T(8,128)(2,1)S(1)} %fusion.20), channel_id=1, replica_groups=mesh['grp'=2,'row'=4,'col'=2,'vec'=2] {'col'}, use_global_device_ids=true, to_apply=%region_16.20 | all-reduce | flops 8192 | bytes 32768 | tf_op jit(solution)/shard_map/psum | solution.py:80
  309.7 3.8 collective-permute-start.41
  315.3 5.5 %collective-permute-done.40 = bf16[32,256]{1,0:T(8,128)(2,1)S(1)} collective-permute-done((bf16[32,256]{1,0:T(8,128)(2,1)S(1)}, bf16[32,256]{1,0:T(8,128)(2,1)S(1)}, u32[]{:S(2)}, u32[]{:S(2)}) %collective-permute-start.40) | collective-permute-done | bytes 16416 | tf_op jit(solution)/shard_map/ppermute | solution.py:25
  322.6 7.0 %psum.148 = bf16[32,256]{1,0:T(8,128)(2,1)S(1)} all-reduce(bf16[32,256]{1,0:T(8,128)(2,1)S(1)} %bitcast.501), channel_id=1, replica_groups=mesh['grp'=2,'row'=4,'col'=2,'vec'=2] {'col'}, use_global_device_ids=true, to_apply=%region_17.21 | all-reduce | flops 8192 | bytes 32768 | tf_op jit(solution)/shard_map/psum | solution.py:80
  329.7 3.8 collective-permute-start.44
  335.3 5.5 %collective-permute-done.43 = bf16[32,256]{1,0:T(8,128)(2,1)S(1)} collective-permute-done((bf16[32,256]{1,0:T(8,128)(2,1)S(1)}, bf16[32,256]{1,0:T(8,128)(2,1)S(1)}, u32[]{:S(2)}, u32[]{:S(2)}) %collective-permute-start.43) | collective-permute-done | bytes 16416 | tf_op jit(solution)/shard_map/ppermute | solution.py:25
  342.6 8.3 %psum.149 = bf16[32,2,128]{2,0,1:T(8,128)(2,1)S(1)} all-reduce(bf16[32,2,128]{2,0,1:T(8,128)(2,1)S(1)} %fusion.18), channel_id=1, replica_groups=mesh['grp'=2,'row'=4,'col'=2,'vec'=2] {'col'}, use_global_device_ids=true, to_apply=%region_18.22 | all-reduce | flops 8192 | bytes 32768 | tf_op jit(solution)/shard_map/psum | solution.py:80
  351.1 3.9 collective-permute-start.47
  356.6 5.5 %collective-permute-done.46 = bf16[32,256]{1,0:T(8,128)(2,1)S(1)} collective-permute-done((bf16[32,256]{1,0:T(8,128)(2,1)S(1)}, bf16[32,256]{1,0:T(8,128)(2,1)S(1)}, u32[]{:S(2)}, u32[]{:S(2)}) %collective-permute-start.46) | collective-permute-done | bytes 16416 | tf_op jit(solution)/shard_map/ppermute | solution.py:25
  363.9 7.0 %psum.150 = bf16[32,256]{1,0:T(8,128)(2,1)S(1)} all-reduce(bf16[32,256]{1,0:T(8,128)(2,1)S(1)} %bitcast.502), channel_id=1, replica_groups=mesh['grp'=2,'row'=4,'col'=2,'vec'=2] {'col'}, use_global_device_ids=true, to_apply=%region_19.23 | all-reduce | flops 8192 | bytes 32768 | tf_op jit(solution)/shard_map/psum | solution.py:80
  371.0 1.8 all_gather.7
  373.0 15.8 %psum.151 = f32[64,64]{0,1:T(8,128)S(1)} all-reduce(f32[64,64]{0,1:T(8,128)S(1)} %fusion.159), channel_id=1, replica_groups=mesh['grp'=2,'row'=4,'col'=2,'vec'=2] {'row'}, use_global_device_ids=true, to_apply=%region_20.24 | all-reduce | flops 4096 | bytes 32768 | tf_op jit(solution)/shard_map/psum | solution.py:51
  388.8 5.8 %cholesky.55 = f32[64,64]{1,0:T(8,128)S(1)} custom-call(f32[64,64]{1,0:T(8,128)S(1)} %fusion.118), custom_call_target="Cholesky" | custom-call | tf_op jit(solution)/shard_map/jit(cholesky)/cholesky | solution.py:52
  396.0 4.9 %custom-call.7 = f32[1,64,64]{1,2,0:T(8,128)S(1)} custom-call(f32[1,64,64]{2,1,0:T(8,128)S(1)} %fusion.102), custom_call_target="InvertDiagBlocksLowerTriangular" | custom-call | tf_op jit(solution)/shard_map/jit(_solve_triangular)/triangular_solve | solution.py:53
  (255 shorter events, 53.6 us)
Async XLA Ops:
  0.0 15.3 %copy-start.2 = (s32[2,32]{1,0:T(2,128)S(1)}, s32[2,32]{1,0:T(2,128)}, u32[]{:S(2)}) copy-start(s32[2,32]{1,0:T(2,128)} %param.11) | copy-start | bytes 772
  0.8 14.9 %collective-permute-start.2 = (bf16[32,256]{1,0:T(8,128)(2,1)S(1)}, bf16[32,256]{1,0:T(8,128)(2,1)S(1)}, u32[]{:S(2)}, u32[]{:S(2)}) collective-permute-start(bf16[32,256]{1,0:T(8,128)(2,1)S(1)} %convert_element_type.271), channel_id=1, source_target_pairs={{4,0},{8,4},{12,8},{0,12},{5,1},{9,5},{13,9},{1,13},{6,2},{10,6},{... | collective-permute-start | bytes 49160 | tf_op jit(solution)/shard_map/ppermute | solution.py:27
  5.8 9.8 %collective-permute-start = (bf16[32,256]{1,0:T(8,128)(2,1)S(1)}, bf16[32,256]{1,0:T(8,128)(2,1)S(1)}, u32[]{:S(2)}, u32[]{:S(2)}) collective-permute-start(bf16[32,256]{1,0:T(8,128)(2,1)S(1)} %convert_element_type.271), channel_id=1, source_target_pairs={{0,4},{4,8},{8,12},{12,0},{1,5},{5,9},{9,13},{13,1},{2,6},{6,10},{... | collective-permute-start | bytes 49160 | tf_op jit(solution)/shard_map/ppermute | solution.py:25
  8.6 13.9 %copy-start.1 = (bf16[2,16,128,128]{3,2,1,0:T(8,128)(2,1)S(1)}, bf16[2,16,128,128]{3,2,1,0:T(8,128)(2,1)}, u32[]{:S(2)}) copy-start(bf16[2,16,128,128]{3,2,1,0:T(8,128)(2,1)} %param.10) | copy-start | bytes 3145732
  15.6 5.6 %collective-permute-start.1 = (bf16[32,256]{1,0:T(8,128)(2,1)S(1)}, bf16[32,256]{1,0:T(8,128)(2,1)S(1)}, u32[]{:S(2)}, u32[]{:S(2)}) collective-permute-start(bf16[32,256]{1,0:T(8,128)(2,1)S(1)} %collective-permute-done), channel_id=1, source_target_pairs={{0,4},{4,8},{8,12},{12,0},{1,5},{5,9},{9,13},{13,1},{2,6},{6,10},{... | collective-permute-start | bytes 49160 | tf_op jit(solution)/shard_map/ppermute | solution.py:25
  31.2 5.6 %collective-permute-start.3 = (bf16[32,256]{1,0:T(8,128)(2,1)S(1)}, bf16[32,256]{1,0:T(8,128)(2,1)S(1)}, u32[]{:S(2)}, u32[]{:S(2)}) collective-permute-start(bf16[32,256]{1,0:T(8,128)(2,1)S(1)} %fusion.123), channel_id=1, source_target_pairs={{0,4},{4,8},{8,12},{12,0},{1,5},{5,9},{9,13},{13,1},{2,6},{6,10},{... | collective-permute-start | bytes 49160 | tf_op jit(solution)/shard_map/ppermute | solution.py:25
  31.3 5.5 %collective-permute-start.5 = (bf16[32,256]{1,0:T(8,128)(2,1)S(1)}, bf16[32,256]{1,0:T(8,128)(2,1)S(1)}, u32[]{:S(2)}, u32[]{:S(2)}) collective-permute-start(bf16[32,256]{1,0:T(8,128)(2,1)S(1)} %fusion.123), channel_id=1, source_target_pairs={{4,0},{8,4},{12,8},{0,12},{5,1},{9,5},{13,9},{1,13},{6,2},{10,6},{... | collective-permute-start | bytes 49160 | tf_op jit(solution)/shard_map/ppermute | solution.py:27
  36.8 5.5 %collective-permute-start.4 = (bf16[32,256]{1,0:T(8,128)(2,1)S(1)}, bf16[32,256]{1,0:T(8,128)(2,1)S(1)}, u32[]{:S(2)}, u32[]{:S(2)}) collective-permute-start(bf16[32,256]{1,0:T(8,128)(2,1)S(1)} %collective-permute-done.3), channel_id=1, source_target_pairs={{0,4},{4,8},{8,12},{12,0},{1,5},{5,9},{9,13},{13,1},{2,6},{6,10},{... | collective-permute-start | bytes 49160 | tf_op jit(solution)/shard_map/ppermute | solution.py:25
  43.6 7.8 %copy-start = (f32[32,256]{1,0:T(8,128)S(1)}, f32[32,256]{1,0:T(8,128)}, u32[]{:S(2)}) copy-start(f32[32,256]{1,0:T(8,128)} %param.9) | copy-start | bytes 98308
  51.4 5.6 %collective-permute-start.6 = (bf16[32,256]{1,0:T(8,128)(2,1)S(1)}, bf16[32,256]{1,0:T(8,128)(2,1)S(1)}, u32[]{:S(2)}, u32[]{:S(2)}) collective-permute-start(bf16[32,256]{1,0:T(8,128)(2,1)S(1)} %fusion.125), channel_id=1, source_target_pairs={{0,4},{4,8},{8,12},{12,0},{1,5},{5,9},{9,13},{13,1},{2,6},{6,10},{... | collective-permute-start | bytes 49160 | tf_op jit(solution)/shard_map/ppermute | solution.py:25
  51.5 5.5 %collective-permute-start.8 = (bf16[32,256]{1,0:T(8,128)(2,1)S(1)}, bf16[32,256]{1,0:T(8,128)(2,1)S(1)}, u32[]{:S(2)}, u32[]{:S(2)}) collective-permute-start(bf16[32,256]{1,0:T(8,128)(2,1)S(1)} %fusion.125), channel_id=1, source_target_pairs={{4,0},{8,4},{12,8},{0,12},{5,1},{9,5},{13,9},{1,13},{6,2},{10,6},{... | collective-permute-start | bytes 49160 | tf_op jit(solution)/shard_map/ppermute | solution.py:27
  57.0 5.5 %collective-permute-start.7 = (bf16[32,256]{1,0:T(8,128)(2,1)S(1)}, bf16[32,256]{1,0:T(8,128)(2,1)S(1)}, u32[]{:S(2)}, u32[]{:S(2)}) collective-permute-start(bf16[32,256]{1,0:T(8,128)(2,1)S(1)} %collective-permute-done.6), channel_id=1, source_target_pairs={{0,4},{4,8},{8,12},{12,0},{1,5},{5,9},{9,13},{13,1},{2,6},{6,10},{... | collective-permute-start | bytes 49160 | tf_op jit(solution)/shard_map/ppermute | solution.py:25
  72.5 5.6 %collective-permute-start.9 = (bf16[32,256]{1,0:T(8,128)(2,1)S(1)}, bf16[32,256]{1,0:T(8,128)(2,1)S(1)}, u32[]{:S(2)}, u32[]{:S(2)}) collective-permute-start(bf16[32,256]{1,0:T(8,128)(2,1)S(1)} %fusion.156), channel_id=1, source_target_pairs={{0,4},{4,8},{8,12},{12,0},{1,5},{5,9},{9,13},{13,1},{2,6},{6,10},{... | collective-permute-start | bytes 49160 | tf_op jit(solution)/shard_map/ppermute | solution.py:25
  72.6 5.6 %collective-permute-start.11 = (bf16[32,256]{1,0:T(8,128)(2,1)S(1)}, bf16[32,256]{1,0:T(8,128)(2,1)S(1)}, u32[]{:S(2)}, u32[]{:S(2)}) collective-permute-start(bf16[32,256]{1,0:T(8,128)(2,1)S(1)} %fusion.156), channel_id=1, source_target_pairs={{4,0},{8,4},{12,8},{0,12},{5,1},{9,5},{13,9},{1,13},{6,2},{10,6},{... | collective-permute-start | bytes 49160 | tf_op jit(solution)/shard_map/ppermute | solution.py:27
  78.1 5.5 %collective-permute-start.10 = (bf16[32,256]{1,0:T(8,128)(2,1)S(1)}, bf16[32,256]{1,0:T(8,128)(2,1)S(1)}, u32[]{:S(2)}, u32[]{:S(2)}) collective-permute-start(bf16[32,256]{1,0:T(8,128)(2,1)S(1)} %collective-permute-done.9), channel_id=1, source_target_pairs={{0,4},{4,8},{8,12},{12,0},{1,5},{5,9},{9,13},{13,1},{2,6},{6,10},{... | collective-permute-start | bytes 49160 | tf_op jit(solution)/shard_map/ppermute | solution.py:25
  92.7 5.6 %collective-permute-start.12 = (bf16[32,256]{1,0:T(8,128)(2,1)S(1)}, bf16[32,256]{1,0:T(8,128)(2,1)S(1)}, u32[]{:S(2)}, u32[]{:S(2)}) collective-permute-start(bf16[32,256]{1,0:T(8,128)(2,1)S(1)} %fusion.155), channel_id=1, source_target_pairs={{0,4},{4,8},{8,12},{12,0},{1,5},{5,9},{9,13},{13,1},{2,6},{6,10},{... | collective-permute-start | bytes 49160 | tf_op jit(solution)/shard_map/ppermute | solution.py:25
  92.8 5.5 %collective-permute-start.14 = (bf16[32,256]{1,0:T(8,128)(2,1)S(1)}, bf16[32,256]{1,0:T(8,128)(2,1)S(1)}, u32[]{:S(2)}, u32[]{:S(2)}) collective-permute-start(bf16[32,256]{1,0:T(8,128)(2,1)S(1)} %fusion.155), channel_id=1, source_target_pairs={{4,0},{8,4},{12,8},{0,12},{5,1},{9,5},{13,9},{1,13},{6,2},{10,6},{... | collective-permute-start | bytes 49160 | tf_op jit(solution)/shard_map/ppermute | solution.py:27
  98.3 5.5 %collective-permute-start.13 = (bf16[32,256]{1,0:T(8,128)(2,1)S(1)}, bf16[32,256]{1,0:T(8,128)(2,1)S(1)}, u32[]{:S(2)}, u32[]{:S(2)}) collective-permute-start(bf16[32,256]{1,0:T(8,128)(2,1)S(1)} %collective-permute-done.12), channel_id=1, source_target_pairs={{0,4},{4,8},{8,12},{12,0},{1,5},{5,9},{9,13},{13,1},{2,6},{6,10},{... | collective-permute-start | bytes 49160 | tf_op jit(solution)/shard_map/ppermute | solution.py:25
  113.9 5.6 %collective-permute-start.15 = (bf16[32,256]{1,0:T(8,128)(2,1)S(1)}, bf16[32,256]{1,0:T(8,128)(2,1)S(1)}, u32[]{:S(2)}, u32[]{:S(2)}) collective-permute-start(bf16[32,256]{1,0:T(8,128)(2,1)S(1)} %fusion.130), channel_id=1, source_target_pairs={{0,4},{4,8},{8,12},{12,0},{1,5},{5,9},{9,13},{13,1},{2,6},{6,10},{... | collective-permute-start | bytes 49160 | tf_op jit(solution)/shard_map/ppermute | solution.py:25
  113.9 5.5 %collective-permute-start.17 = (bf16[32,256]{1,0:T(8,128)(2,1)S(1)}, bf16[32,256]{1,0:T(8,128)(2,1)S(1)}, u32[]{:S(2)}, u32[]{:S(2)}) collective-permute-start(bf16[32,256]{1,0:T(8,128)(2,1)S(1)} %fusion.130), channel_id=1, source_target_pairs={{4,0},{8,4},{12,8},{0,12},{5,1},{9,5},{13,9},{1,13},{6,2},{10,6},{... | collective-permute-start | bytes 49160 | tf_op jit(solution)/shard_map/ppermute | solution.py:27
  119.5 5.5 %collective-permute-start.16 = (bf16[32,256]{1,0:T(8,128)(2,1)S(1)}, bf16[32,256]{1,0:T(8,128)(2,1)S(1)}, u32[]{:S(2)}, u32[]{:S(2)}) collective-permute-start(bf16[32,256]{1,0:T(8,128)(2,1)S(1)} %collective-permute-done.15), channel_id=1, source_target_pairs={{0,4},{4,8},{8,12},{12,0},{1,5},{5,9},{9,13},{13,1},{2,6},{6,10},{... | collective-permute-start | bytes 49160 | tf_op jit(solution)/shard_map/ppermute | solution.py:25
  134.0 5.6 %collective-permute-start.18 = (bf16[32,256]{1,0:T(8,128)(2,1)S(1)}, bf16[32,256]{1,0:T(8,128)(2,1)S(1)}, u32[]{:S(2)}, u32[]{:S(2)}) collective-permute-start(bf16[32,256]{1,0:T(8,128)(2,1)S(1)} %fusion.126), channel_id=1, source_target_pairs={{0,4},{4,8},{8,12},{12,0},{1,5},{5,9},{9,13},{13,1},{2,6},{6,10},{... | collective-permute-start | bytes 49160 | tf_op jit(solution)/shard_map/ppermute | solution.py:25
  134.1 5.5 %collective-permute-start.20 = (bf16[32,256]{1,0:T(8,128)(2,1)S(1)}, bf16[32,256]{1,0:T(8,128)(2,1)S(1)}, u32[]{:S(2)}, u32[]{:S(2)}) collective-permute-start(bf16[32,256]{1,0:T(8,128)(2,1)S(1)} %fusion.126), channel_id=1, source_target_pairs={{4,0},{8,4},{12,8},{0,12},{5,1},{9,5},{13,9},{1,13},{6,2},{10,6},{... | collective-permute-start | bytes 49160 | tf_op jit(solution)/shard_map/ppermute | solution.py:27
  139.6 5.5 %collective-permute-start.19 = (bf16[32,256]{1,0:T(8,128)(2,1)S(1)}, bf16[32,256]{1,0:T(8,128)(2,1)S(1)}, u32[]{:S(2)}, u32[]{:S(2)}) collective-permute-start(bf16[32,256]{1,0:T(8,128)(2,1)S(1)} %collective-permute-done.18), channel_id=1, source_target_pairs={{0,4},{4,8},{8,12},{12,0},{1,5},{5,9},{9,13},{13,1},{2,6},{6,10},{... | collective-permute-start | bytes 49160 | tf_op jit(solution)/shard_map/ppermute | solution.py:25
  155.2 5.6 %collective-permute-start.21 = (bf16[32,256]{1,0:T(8,128)(2,1)S(1)}, bf16[32,256]{1,0:T(8,128)(2,1)S(1)}, u32[]{:S(2)}, u32[]{:S(2)}) collective-permute-start(bf16[32,256]{1,0:T(8,128)(2,1)S(1)} %fusion.112), channel_id=1, source_target_pairs={{0,4},{4,8},{8,12},{12,0},{1,5},{5,9},{9,13},{13,1},{2,6},{6,10},{... | collective-permute-start | bytes 49160 | tf_op jit(solution)/shard_map/ppermute | solution.py:25
  155.3 5.5 %collective-permute-start.23 = (bf16[32,256]{1,0:T(8,128)(2,1)S(1)}, bf16[32,256]{1,0:T(8,128)(2,1)S(1)}, u32[]{:S(2)}, u32[]{:S(2)}) collective-permute-start(bf16[32,256]{1,0:T(8,128)(2,1)S(1)} %fusion.112), channel_id=1, source_target_pairs={{4,0},{8,4},{12,8},{0,12},{5,1},{9,5},{13,9},{1,13},{6,2},{10,6},{... | collective-permute-start | bytes 49160 | tf_op jit(solution)/shard_map/ppermute | solution.py:27
  160.8 5.5 %collective-permute-start.22 = (bf16[32,256]{1,0:T(8,128)(2,1)S(1)}, bf16[32,256]{1,0:T(8,128)(2,1)S(1)}, u32[]{:S(2)}, u32[]{:S(2)}) collective-permute-start(bf16[32,256]{1,0:T(8,128)(2,1)S(1)} %collective-permute-done.21), channel_id=1, source_target_pairs={{0,4},{4,8},{8,12},{12,0},{1,5},{5,9},{9,13},{13,1},{2,6},{6,10},{... | collective-permute-start | bytes 49160 | tf_op jit(solution)/shard_map/ppermute | solution.py:25
  205.6 5.6 %collective-permute-start.24 = (bf16[32,256]{1,0:T(8,128)(2,1)S(1)}, bf16[32,256]{1,0:T(8,128)(2,1)S(1)}, u32[]{:S(2)}, u32[]{:S(2)}) collective-permute-start(bf16[32,256]{1,0:T(8,128)(2,1)S(1)} %dynamic-slice_convert_fusion), channel_id=1, source_target_pairs={{0,4},{4,8},{8,12},{12,0},{1,5},{5,9},{9,13},{13,1},{2,6},{6,10},{... | collective-permute-start | bytes 49160 | tf_op jit(solution)/shard_map/ppermute | solution.py:25
  205.7 5.5 %collective-permute-start.26 = (bf16[32,256]{1,0:T(8,128)(2,1)S(1)}, bf16[32,256]{1,0:T(8,128)(2,1)S(1)}, u32[]{:S(2)}, u32[]{:S(2)}) collective-permute-start(bf16[32,256]{1,0:T(8,128)(2,1)S(1)} %dynamic-slice_convert_fusion), channel_id=1, source_target_pairs={{4,0},{8,4},{12,8},{0,12},{5,1},{9,5},{13,9},{1,13},{6,2},{10,6},{... | collective-permute-start | bytes 49160 | tf_op jit(solution)/shard_map/ppermute | solution.py:27
  211.2 5.5 %collective-permute-start.25 = (bf16[32,256]{1,0:T(8,128)(2,1)S(1)}, bf16[32,256]{1,0:T(8,128)(2,1)S(1)}, u32[]{:S(2)}, u32[]{:S(2)}) collective-permute-start(bf16[32,256]{1,0:T(8,128)(2,1)S(1)} %collective-permute-done.24), channel_id=1, source_target_pairs={{0,4},{4,8},{8,12},{12,0},{1,5},{5,9},{9,13},{13,1},{2,6},{6,10},{... | collective-permute-start | bytes 49160 | tf_op jit(solution)/shard_map/ppermute | solution.py:25
  226.7 5.8 %collective-permute-start.27 = (bf16[32,256]{1,0:T(8,128)(2,1)S(1)}, bf16[32,256]{1,0:T(8,128)(2,1)S(1)}, u32[]{:S(2)}, u32[]{:S(2)}) collective-permute-start(bf16[32,256]{1,0:T(8,128)(2,1)S(1)} %fusion.124), channel_id=1, source_target_pairs={{0,4},{4,8},{8,12},{12,0},{1,5},{5,9},{9,13},{13,1},{2,6},{6,10},{... | collective-permute-start | bytes 49160 | tf_op jit(solution)/shard_map/ppermute | solution.py:25
  227.0 5.5 %collective-permute-start.29 = (bf16[32,256]{1,0:T(8,128)(2,1)S(1)}, bf16[32,256]{1,0:T(8,128)(2,1)S(1)}, u32[]{:S(2)}, u32[]{:S(2)}) collective-permute-start(bf16[32,256]{1,0:T(8,128)(2,1)S(1)} %fusion.124), channel_id=1, source_target_pairs={{4,0},{8,4},{12,8},{0,12},{5,1},{9,5},{13,9},{1,13},{6,2},{10,6},{... | collective-permute-start | bytes 49160 | tf_op jit(solution)/shard_map/ppermute | solution.py:27
  232.5 5.5 %collective-permute-start.28 = (bf16[32,256]{1,0:T(8,128)(2,1)S(1)}, bf16[32,256]{1,0:T(8,128)(2,1)S(1)}, u32[]{:S(2)}, u32[]{:S(2)}) collective-permute-start(bf16[32,256]{1,0:T(8,128)(2,1)S(1)} %collective-permute-done.27), channel_id=1, source_target_pairs={{0,4},{4,8},{8,12},{12,0},{1,5},{5,9},{9,13},{13,1},{2,6},{6,10},{... | collective-permute-start | bytes 49160 | tf_op jit(solution)/shard_map/ppermute | solution.py:25
  247.0 5.6 %collective-permute-start.30 = (bf16[32,256]{1,0:T(8,128)(2,1)S(1)}, bf16[32,256]{1,0:T(8,128)(2,1)S(1)}, u32[]{:S(2)}, u32[]{:S(2)}) collective-permute-start(bf16[32,256]{1,0:T(8,128)(2,1)S(1)} %fusion.154), channel_id=1, source_target_pairs={{0,4},{4,8},{8,12},{12,0},{1,5},{5,9},{9,13},{13,1},{2,6},{6,10},{... | collective-permute-start | bytes 49160 | tf_op jit(solution)/shard_map/ppermute | solution.py:25
  247.1 5.5 %collective-permute-start.32 = (bf16[32,256]{1,0:T(8,128)(2,1)S(1)}, bf16[32,256]{1,0:T(8,128)(2,1)S(1)}, u32[]{:S(2)}, u32[]{:S(2)}) collective-permute-start(bf16[32,256]{1,0:T(8,128)(2,1)S(1)} %fusion.154), channel_id=1, source_target_pairs={{4,0},{8,4},{12,8},{0,12},{5,1},{9,5},{13,9},{1,13},{6,2},{10,6},{... | collective-permute-start | bytes 49160 | tf_op jit(solution)/shard_map/ppermute | solution.py:27
  252.6 5.5 %collective-permute-start.31 = (bf16[32,256]{1,0:T(8,128)(2,1)S(1)}, bf16[32,256]{1,0:T(8,128)(2,1)S(1)}, u32[]{:S(2)}, u32[]{:S(2)}) collective-permute-start(bf16[32,256]{1,0:T(8,128)(2,1)S(1)} %collective-permute-done.30), channel_id=1, source_target_pairs={{0,4},{4,8},{8,12},{12,0},{1,5},{5,9},{9,13},{13,1},{2,6},{6,10},{... | collective-permute-start | bytes 49160 | tf_op jit(solution)/shard_map/ppermute | solution.py:25
  268.3 5.6 %collective-permute-start.33 = (bf16[32,256]{1,0:T(8,128)(2,1)S(1)}, bf16[32,256]{1,0:T(8,128)(2,1)S(1)}, u32[]{:S(2)}, u32[]{:S(2)}) collective-permute-start(bf16[32,256]{1,0:T(8,128)(2,1)S(1)} %fusion.157), channel_id=1, source_target_pairs={{0,4},{4,8},{8,12},{12,0},{1,5},{5,9},{9,13},{13,1},{2,6},{6,10},{... | collective-permute-start | bytes 49160 | tf_op jit(solution)/shard_map/ppermute | solution.py:25
  268.4 5.5 %collective-permute-start.35 = (bf16[32,256]{1,0:T(8,128)(2,1)S(1)}, bf16[32,256]{1,0:T(8,128)(2,1)S(1)}, u32[]{:S(2)}, u32[]{:S(2)}) collective-permute-start(bf16[32,256]{1,0:T(8,128)(2,1)S(1)} %fusion.157), channel_id=1, source_target_pairs={{4,0},{8,4},{12,8},{0,12},{5,1},{9,5},{13,9},{1,13},{6,2},{10,6},{... | collective-permute-start | bytes 49160 | tf_op jit(solution)/shard_map/ppermute | solution.py:27
  273.9 5.5 %collective-permute-start.34 = (bf16[32,256]{1,0:T(8,128)(2,1)S(1)}, bf16[32,256]{1,0:T(8,128)(2,1)S(1)}, u32[]{:S(2)}, u32[]{:S(2)}) collective-permute-start(bf16[32,256]{1,0:T(8,128)(2,1)S(1)} %collective-permute-done.33), channel_id=1, source_target_pairs={{0,4},{4,8},{8,12},{12,0},{1,5},{5,9},{9,13},{13,1},{2,6},{6,10},{... | collective-permute-start | bytes 49160 | tf_op jit(solution)/shard_map/ppermute | solution.py:25
  288.4 5.6 %collective-permute-start.36 = (bf16[32,256]{1,0:T(8,128)(2,1)S(1)}, bf16[32,256]{1,0:T(8,128)(2,1)S(1)}, u32[]{:S(2)}, u32[]{:S(2)}) collective-permute-start(bf16[32,256]{1,0:T(8,128)(2,1)S(1)} %fusion.127), channel_id=1, source_target_pairs={{0,4},{4,8},{8,12},{12,0},{1,5},{5,9},{9,13},{13,1},{2,6},{6,10},{... | collective-permute-start | bytes 49160 | tf_op jit(solution)/shard_map/ppermute | solution.py:25
  288.4 5.5 %collective-permute-start.38 = (bf16[32,256]{1,0:T(8,128)(2,1)S(1)}, bf16[32,256]{1,0:T(8,128)(2,1)S(1)}, u32[]{:S(2)}, u32[]{:S(2)}) collective-permute-start(bf16[32,256]{1,0:T(8,128)(2,1)S(1)} %fusion.127), channel_id=1, source_target_pairs={{4,0},{8,4},{12,8},{0,12},{5,1},{9,5},{13,9},{1,13},{6,2},{10,6},{... | collective-permute-start | bytes 49160 | tf_op jit(solution)/shard_map/ppermute | solution.py:27
  294.0 5.5 %collective-permute-start.37 = (bf16[32,256]{1,0:T(8,128)(2,1)S(1)}, bf16[32,256]{1,0:T(8,128)(2,1)S(1)}, u32[]{:S(2)}, u32[]{:S(2)}) collective-permute-start(bf16[32,256]{1,0:T(8,128)(2,1)S(1)} %collective-permute-done.36), channel_id=1, source_target_pairs={{0,4},{4,8},{8,12},{12,0},{1,5},{5,9},{9,13},{13,1},{2,6},{6,10},{... | collective-permute-start | bytes 49160 | tf_op jit(solution)/shard_map/ppermute | solution.py:25
  309.6 5.6 %collective-permute-start.39 = (bf16[32,256]{1,0:T(8,128)(2,1)S(1)}, bf16[32,256]{1,0:T(8,128)(2,1)S(1)}, u32[]{:S(2)}, u32[]{:S(2)}) collective-permute-start(bf16[32,256]{1,0:T(8,128)(2,1)S(1)} %fusion.131), channel_id=1, source_target_pairs={{0,4},{4,8},{8,12},{12,0},{1,5},{5,9},{9,13},{13,1},{2,6},{6,10},{... | collective-permute-start | bytes 49160 | tf_op jit(solution)/shard_map/ppermute | solution.py:25
  309.7 5.5 %collective-permute-start.41 = (bf16[32,256]{1,0:T(8,128)(2,1)S(1)}, bf16[32,256]{1,0:T(8,128)(2,1)S(1)}, u32[]{:S(2)}, u32[]{:S(2)}) collective-permute-start(bf16[32,256]{1,0:T(8,128)(2,1)S(1)} %fusion.131), channel_id=1, source_target_pairs={{4,0},{8,4},{12,8},{0,12},{5,1},{9,5},{13,9},{1,13},{6,2},{10,6},{... | collective-permute-start | bytes 49160 | tf_op jit(solution)/shard_map/ppermute | solution.py:27
  315.2 5.5 %collective-permute-start.40 = (bf16[32,256]{1,0:T(8,128)(2,1)S(1)}, bf16[32,256]{1,0:T(8,128)(2,1)S(1)}, u32[]{:S(2)}, u32[]{:S(2)}) collective-permute-start(bf16[32,256]{1,0:T(8,128)(2,1)S(1)} %collective-permute-done.39), channel_id=1, source_target_pairs={{0,4},{4,8},{8,12},{12,0},{1,5},{5,9},{9,13},{13,1},{2,6},{6,10},{... | collective-permute-start | bytes 49160 | tf_op jit(solution)/shard_map/ppermute | solution.py:25
  329.7 5.6 %collective-permute-start.42 = (bf16[32,256]{1,0:T(8,128)(2,1)S(1)}, bf16[32,256]{1,0:T(8,128)(2,1)S(1)}, u32[]{:S(2)}, u32[]{:S(2)}) collective-permute-start(bf16[32,256]{1,0:T(8,128)(2,1)S(1)} %fusion.132), channel_id=1, source_target_pairs={{0,4},{4,8},{8,12},{12,0},{1,5},{5,9},{9,13},{13,1},{2,6},{6,10},{... | collective-permute-start | bytes 49160 | tf_op jit(solution)/shard_map/ppermute | solution.py:25
  329.7 5.5 %collective-permute-start.44 = (bf16[32,256]{1,0:T(8,128)(2,1)S(1)}, bf16[32,256]{1,0:T(8,128)(2,1)S(1)}, u32[]{:S(2)}, u32[]{:S(2)}) collective-permute-start(bf16[32,256]{1,0:T(8,128)(2,1)S(1)} %fusion.132), channel_id=1, source_target_pairs={{4,0},{8,4},{12,8},{0,12},{5,1},{9,5},{13,9},{1,13},{6,2},{10,6},{... | collective-permute-start | bytes 49160 | tf_op jit(solution)/shard_map/ppermute | solution.py:27
  335.3 5.5 %collective-permute-start.43 = (bf16[32,256]{1,0:T(8,128)(2,1)S(1)}, bf16[32,256]{1,0:T(8,128)(2,1)S(1)}, u32[]{:S(2)}, u32[]{:S(2)}) collective-permute-start(bf16[32,256]{1,0:T(8,128)(2,1)S(1)} %collective-permute-done.42), channel_id=1, source_target_pairs={{0,4},{4,8},{8,12},{12,0},{1,5},{5,9},{9,13},{13,1},{2,6},{6,10},{... | collective-permute-start | bytes 49160 | tf_op jit(solution)/shard_map/ppermute | solution.py:25
  351.0 5.6 %collective-permute-start.45 = (bf16[32,256]{1,0:T(8,128)(2,1)S(1)}, bf16[32,256]{1,0:T(8,128)(2,1)S(1)}, u32[]{:S(2)}, u32[]{:S(2)}) collective-permute-start(bf16[32,256]{1,0:T(8,128)(2,1)S(1)} %fusion.105), channel_id=1, source_target_pairs={{0,4},{4,8},{8,12},{12,0},{1,5},{5,9},{9,13},{13,1},{2,6},{6,10},{... | collective-permute-start | bytes 49160 | tf_op jit(solution)/shard_map/ppermute | solution.py:25
  351.1 5.5 %collective-permute-start.47 = (bf16[32,256]{1,0:T(8,128)(2,1)S(1)}, bf16[32,256]{1,0:T(8,128)(2,1)S(1)}, u32[]{:S(2)}, u32[]{:S(2)}) collective-permute-start(bf16[32,256]{1,0:T(8,128)(2,1)S(1)} %fusion.105), channel_id=1, source_target_pairs={{4,0},{8,4},{12,8},{0,12},{5,1},{9,5},{13,9},{1,13},{6,2},{10,6},{... | collective-permute-start | bytes 49160 | tf_op jit(solution)/shard_map/ppermute | solution.py:27
  356.6 5.5 %collective-permute-start.46 = (bf16[32,256]{1,0:T(8,128)(2,1)S(1)}, bf16[32,256]{1,0:T(8,128)(2,1)S(1)}, u32[]{:S(2)}, u32[]{:S(2)}) collective-permute-start(bf16[32,256]{1,0:T(8,128)(2,1)S(1)} %collective-permute-done.45), channel_id=1, source_target_pairs={{0,4},{4,8},{8,12},{12,0},{1,5},{5,9},{9,13},{13,1},{2,6},{6,10},{... | collective-permute-start | bytes 49160 | tf_op jit(solution)/shard_map/ppermute | solution.py:25
